TPU v7x, 32 devices: a whole 2x2x4 slice. The times are simulated.
32 devices in a mesh: row: 16 (over z, x, core), col: 2 (over y).
Axes of the slice: x: 2, y: 2, z: 4, core: 2. Of those that a mesh axis runs over, the one named last changes fastest.
Arguments:
- counts: int32 [3072, 3072], P('row', 'col'), may hold values from 0 to 3
- theta: bfloat16 [3072, 64], P(('row', 'col')), may hold values from 0.099609375 to 1
- phi: bfloat16 [3072, 64], P(('col', 'row')), may hold values from 0.099609375 to 1
- affinity: float32 [64, 64], replicated, may hold values from 0.0003 to 0.003
Outputs:
- theta_grad: float32 [3072, 64], P(('row', 'col'))
- phi_grad: float32 [3072, 64], P(('col', 'row'))
- affinity_grad: float32 [64, 64], replicated
All inputs are finite; a program needn't handle non-finite values.
Results may differ from a plain program's by a relative error of at most 0.0003.
Values may be sent and summed in bfloat16 or wider, within the bound.
No kernel may reach another device: no remote copies, remote signals or barrier semaphores. Data moves between devices by JAX's collectives and lax.ppermute only.
A program may use at most 64 MiB of HBM per device.

v0:
```python
import jax
import jax.numpy as jnp
from jax import lax
from jax.sharding import PartitionSpec as P


def shards(counts, theta, phi, affinity):
    nodes = theta.shape[0] * lax.axis_size("row") * lax.axis_size("col")
    inverse = 1.0 / nodes
    theta_rows = lax.all_gather(theta, "col", axis=0, tiled=True)
    row_factor = jnp.dot(theta_rows.astype(jnp.float32), affinity, precision=lax.Precision.HIGHEST)
    factor_half = row_factor.astype(jnp.bfloat16)
    members = lax.all_gather(phi, "row", axis=0, tiled=True)
    rate = jnp.dot(row_factor, members.astype(jnp.float32).T, precision=lax.Precision.HIGHEST)
    ratio = (1.0 - counts.astype(jnp.float32) / rate).astype(jnp.bfloat16)
    gphi = jnp.dot(ratio, members, preferred_element_type=jnp.float32)
    phi_sum = lax.psum_scatter(
        lax.dot_general(
            ratio, factor_half, (((0,), (0,)), ((), ())), preferred_element_type=jnp.float32
        ),
        "row",
        scatter_dimension=0,
        tiled=True,
    )
    gphi_sum = lax.psum_scatter(gphi, "col", scatter_dimension=0, tiled=True)
    theta_grad = inverse * jnp.dot(gphi_sum, affinity.T, precision=lax.Precision.HIGHEST)
    phi_grad = inverse * phi_sum
    affinity_part = jnp.dot(theta.astype(jnp.float32).T, gphi_sum, precision=lax.Precision.HIGHEST)
    affinity_grad = inverse * inverse * lax.psum(affinity_part, ("row", "col"))
    return (theta_grad, phi_grad, affinity_grad)


def solution(mesh):
    placed = (P("row", "col"), P(("row", "col"), None), P(("col", "row"), None), P())
    return jax.shard_map(
        shards,
        mesh=mesh,
        in_specs=placed,
        out_specs=(P(("row", "col"), None), P(("col", "row"), None), P()),
        check_vma=False,
    )
```

profile of v0, /device:TPU:0, one launch (start us, length us, event | category | flops | bytes accessed | tf_op | source)
XLA Modules:
  0.0 114.5 jit_solution(16224483972441247521)
XLA Ops:
  7.2 0.0 copy-start
  7.2 0.0 copy-start.2
  7.2 0.0 reduce-scatter.7.cloned.1.call-start
  7.2 5.7 %all-gather = bf16[2,96,64]{1,2,0:T(8,128)(2,1)S(1)} all-gather(bf16[1,96,64]{1,2,0:T(8,128)(2,1)} %bitcast.21), channel_id=1, replica_groups=mesh['row'=16,'col'=2] {'col'}, dimensions={0}, use_global_device_ids=true | all-gather | bytes 36864 | tf_op jit(solution)/shard_map/all_gather | solution.py:10
  13.0 0.1 reshape.7
  13.1 23.0 %all-gather.1 = bf16[16,96,64]{1,2,0:T(8,128)(2,1)S(1)} all-gather(bf16[1,96,64]{1,2,0:T(8,128)(2,1)} %bitcast.22), channel_id=1, replica_groups=mesh['row'=16,'col'=2] {'row'}, dimensions={0}, use_global_device_ids=true | all-gather | bytes 208896 | tf_op jit(solution)/shard_map/all_gather | solution.py:13
  36.2 0.2 copy.12
  36.3 0.3 reshape.9
  36.6 0.0 copy-done
  36.6 0.2 fusion.4
  36.8 0.7 fusion.1
  37.6 0.9 fusion.5
  38.5 0.0 reduce-scatter.7.cloned.1.call-update
  38.6 0.0 reduce-scatter.9.cloned.1.call-start
  38.6 1.3 %fusion.2 = f32[1536,64]{1,0:T(8,128)} fusion(bf16[192,1536]{1,0:T(8,128)(2,1)S(1)} %fusion.1, f32[192,64]{0,1:T(8,128)S(1)} %fusion.4), kind=kOutput, calls=%fused_computation.5 | convolution fusion | flops 37761024 | bytes 1032192
  39.9 0.0 reduce-scatter.9.cloned.1.call-update
  40.0 6.1 %reduce-scatter.7.cloned.1.call-done = f32[96,64]{1,0:T(8,128)} async-done(((f32[192,64]{1,0:T(8,128)}), f32[96,64]{1,0:T(8,128)}) %reduce-scatter.7.cloned.1.call-update) | async-done | bytes 24592
  46.0 1.0 convolution_bitcast_fusion
  47.0 39.5 %psum.7 = f32[64,64]{0,1:T(8,128)S(1)} all-reduce(f32[64,64]{0,1:T(8,128)S(1)} %convolution_bitcast_fusion), channel_id=1, replica_groups=mesh['row'=16,'col'=2] {'row','col'}, use_global_device_ids=true, to_apply=%region_2.0 | all-reduce | flops 4096 | bytes 32768 | tf_op jit(solution)/shard_map/psum | solution.py:29
  86.6 0.7 copy.13
  87.3 1.6 %convolution_multiply_fusion = f32[96,64]{0,1:T(8,128)} fusion(f32[96,64]{1,0:T(8,128)} %reduce-scatter.7.cloned.1.call-done, f32[64,64]{1,0:T(8,128)S(1)} %copy-done), kind=kOutput, calls=%fused_computation.4 | convolution fusion | flops 4724736 | bytes 65536 | tf_op jit(solution)/shard_map/dot_general | solution.py:26
  88.9 17.3 %reduce-scatter.9.cloned.1.call-done = f32[96,64]{1,0:T(8,128)} async-done(((f32[1536,64]{1,0:T(8,128)}), f32[96,64]{1,0:T(8,128)}) %reduce-scatter.9.cloned.1.call-update) | async-done | bytes 24592
  106.2 0.9 copy.17
  107.0 0.6 broadcast_multiply_fusion.1
  (5 shorter events, 0.0 us)
Async XLA Ops:
  7.2 29.4 %copy-start = (f32[64,64]{1,0:T(8,128)S(1)}, f32[64,64]{1,0:T(8,128)}, u32[]{:S(2)}) copy-start(f32[64,64]{1,0:T(8,128)} %param.7) | copy-start | bytes 49156
  7.2 29.7 %copy-start.2 = (s32[192,1536]{1,0:T(8,128)S(1)}, s32[192,1536]{1,0:T(8,128)}, u32[]{:S(2)}) copy-start(s32[192,1536]{1,0:T(8,128)} %param.4) | copy-start | bytes 3538948
  7.2 38.8 %reduce-scatter.7.cloned.1.call-start = ((), (), s32[]{:S(2)}) async-start(), calls=%async_computation.2 | async-start | bytes 147456
  38.5 7.5 %copy-start.1 = (bf16[96,64]{0,1:T(8,128)(2,1)S(1)}, bf16[96,64]{0,1:T(8,128)(2,1)}, u32[]{:S(2)}) copy-start(bf16[96,64]{0,1:T(8,128)(2,1)} %param.5) | copy-start | bytes 36868
  38.6 67.6 %reduce-scatter.9.cloned.1.call-start = ((), (), s32[]{:S(2)}) async-start(), calls=%async_computation.3 | async-start | bytes 835584
Sparse Core Ops, SparseCore 0:
  38.7 7.2 reduce-scatter.6
  49.6 56.5 reduce-scatter.8
where the time goes:
time: 115 us; the launch traced here: 114 us
  blocking collectives  68.3 us (59%)
  waiting for transfers between devices  23.3 us (20%)
  between operations  14.1 us (12%)
  matrix products  5.89 us (5%)
  local copies, waits for them, and re-layouts  2.15 us (2%)
    psum x1, blocking collectives, shards(): affinity_grad = inverse * inverse * lax.psum(affinity_part, ('row', 'col'))  39.5 us
    unnamed x4, waiting for transfers between devices  23.3 us
    all_gather x1, blocking collectives, shards(): members = lax.all_gather(phi, 'row', axis=0, tiled=True)  23 us
    all_gather x1, blocking collectives, shards(): theta_rows = lax.all_gather(theta, 'col', axis=0, tiled=True)  5.75 us
  transfers between devices with their start and end apart: 2, of which 2 were waited for; matrix products, arithmetic and copies ran while one was open for 4% of the time, Pallas kernels for 0%

commit v1 on v0

--- a/solution.py
+++ b/solution.py
@@ -26,7 +26,9 @@
     theta_grad = inverse * jnp.dot(gphi_sum, affinity.T, precision=lax.Precision.HIGHEST)
     phi_grad = inverse * phi_sum
     affinity_part = jnp.dot(theta.astype(jnp.float32).T, gphi_sum, precision=lax.Precision.HIGHEST)
-    affinity_grad = inverse * inverse * lax.psum(affinity_part, ("row", "col"))
+    affinity_grad = (
+        inverse * inverse * jax.lax.all_gather(affinity_part, ("row", "col")).sum(axis=0)
+    )
     return (theta_grad, phi_grad, affinity_grad)
 
 

time: 115 us -> 131 us (1.14)
  blocking collectives: 68.3 us -> 102 us
  waiting for transfers between devices: 23.3 us -> 6.09 us
    all_gather x0 -> x1, blocking collectives: none -> 73.3 us  [shards(): jax.lax.all_gather(affinity_part, ('row', 'col')).sum(axis=0)]
    psum x1 -> x0, blocking collectives: 39.5 us -> none  [shards(): affinity_grad = inverse * inverse * lax.psum(affinity_part, ('row', 'col'))]
    unnamed x4, waiting for transfers between devices: 23.3 us -> 6.09 us
  transfers between devices with their start and end apart: 2 -> 2, of which waited for: 2 -> 1; matrix products, arithmetic and copies ran while one was open for 4% -> 3% of each run, Pallas kernels for 0% -> 0%
where the time goes in v1:
time: 131 us; the launch traced here: 130 us
  blocking collectives  102 us (78%)
  between operations  14.1 us (11%)
  waiting for transfers between devices  6.09 us (5%)
  matrix products  5.09 us (4%)
  local copies, waits for them, and re-layouts  2.3 us (2%)
    all_gather x1, blocking collectives, shards(): jax.lax.all_gather(affinity_part, ('row', 'col')).sum(axis=0)  73.3 us
    all_gather x1, blocking collectives, shards(): members = lax.all_gather(phi, 'row', axis=0, tiled=True)  23 us
    unnamed x4, waiting for transfers between devices  6.09 us
    all_gather x1, blocking collectives, shards(): theta_rows = lax.all_gather(theta, 'col', axis=0, tiled=True)  5.75 us
  transfers between devices with their start and end apart: 2, of which 1 were waited for; matrix products, arithmetic and copies ran while one was open for 3% of the time, Pallas kernels for 0%

profile of v1, /device:TPU:0, one launch (start us, length us, event | category | flops | bytes accessed | tf_op | source)
XLA Modules:
  0.0 130.4 jit_solution(4352712040459780495)
XLA Ops:
  7.2 0.0 copy-start
  7.2 0.0 reduce-scatter.7.cloned.1.call-start
  7.2 5.7 %all-gather.1 = bf16[2,96,64]{1,2,0:T(8,128)(2,1)S(1)} all-gather(bf16[1,96,64]{1,2,0:T(8,128)(2,1)} %bitcast.23), channel_id=1, replica_groups=mesh['row'=16,'col'=2] {'col'}, dimensions={0}, use_global_device_ids=true | all-gather | bytes 36864 | tf_op jit(solution)/shard_map/all_gather | solution.py:10
  13.0 0.1 reshape.8
  13.1 23.0 %all-gather.2 = bf16[16,96,64]{1,2,0:T(8,128)(2,1)S(1)} all-gather(bf16[1,96,64]{1,2,0:T(8,128)(2,1)} %bitcast.24), channel_id=1, replica_groups=mesh['row'=16,'col'=2] {'row'}, dimensions={0}, use_global_device_ids=true | all-gather | bytes 208896 | tf_op jit(solution)/shard_map/all_gather | solution.py:13
  36.2 0.2 copy.10
  36.3 0.3 reshape.10
  36.6 0.2 fusion.4
  36.8 0.7 fusion.1
  37.6 0.9 fusion.5
  38.5 0.0 reduce-scatter.7.cloned.1.call-update
  38.6 0.0 reduce-scatter.9.cloned.1.call-start
  38.6 1.3 %fusion.2 = f32[1536,64]{1,0:T(8,128)} fusion(bf16[192,1536]{1,0:T(8,128)(2,1)S(1)} %fusion.1, f32[192,64]{0,1:T(8,128)S(1)} %fusion.4), kind=kOutput, calls=%fused_computation.5 | convolution fusion | flops 37761024 | bytes 1032192
  39.9 0.0 reduce-scatter.9.cloned.1.call-update
  40.0 6.1 %reduce-scatter.7.cloned.1.call-done = f32[96,64]{1,0:T(8,128)} async-done(((f32[192,64]{1,0:T(8,128)}), f32[96,64]{1,0:T(8,128)}) %reduce-scatter.7.cloned.1.call-update) | async-done | bytes 24592
  46.0 1.0 convolution_bitcast_fusion
  47.0 0.1 copy.11
  47.1 73.3 %all-gather = f32[2048,64]{1,0:T(8,128)S(1)} all-gather(f32[64,64]{1,0:T(8,128)S(1)} %copy.11), channel_id=2, replica_groups=mesh['row'=16,'col'=2] {'row','col'}, dimensions={0}, use_global_device_ids=true | all-gather | bytes 540672 | tf_op jit(solution)/shard_map/all_gather | solution.py:30
  120.4 0.1 reduce_sum.9
  120.5 0.1 copy.18
  120.6 0.7 copy.13
  121.3 0.8 convolution_multiply_fusion
  122.1 0.9 copy.17
  123.0 0.6 broadcast_multiply_fusion.1
  (10 shorter events, 0.1 us)
Async XLA Ops:
  7.2 29.4 %copy-start = (f32[64,64]{1,0:T(8,128)S(1)}, f32[64,64]{1,0:T(8,128)}, u32[]{:S(2)}) copy-start(f32[64,64]{1,0:T(8,128)} %param.7) | copy-start | bytes 49156
  7.2 29.7 %copy-start.3 = (s32[192,1536]{1,0:T(8,128)S(1)}, s32[192,1536]{1,0:T(8,128)}, u32[]{:S(2)}) copy-start(s32[192,1536]{1,0:T(8,128)} %param.4) | copy-start | bytes 3538948
  7.2 38.8 %reduce-scatter.7.cloned.1.call-start = ((), (), s32[]{:S(2)}) async-start(), calls=%async_computation.2 | async-start | bytes 147456
  38.5 7.5 %copy-start.2 = (bf16[96,64]{0,1:T(8,128)(2,1)S(1)}, bf16[96,64]{0,1:T(8,128)(2,1)}, u32[]{:S(2)}) copy-start(bf16[96,64]{0,1:T(8,128)(2,1)} %param.5) | copy-start | bytes 36868
  38.6 83.5 %reduce-scatter.9.cloned.1.call-start = ((), (), s32[]{:S(2)}) async-start(), calls=%async_computation.3 | async-start | bytes 835584
  47.1 74.1 %copy-start.1 = (f32[96,64]{1,0:T(8,128)S(1)}, f32[96,64]{1,0:T(8,128)}, u32[]{:S(2)}) copy-start(f32[96,64]{1,0:T(8,128)} %reduce-scatter.7.cloned.1.call-done) | copy-start | bytes 73732
Sparse Core Ops, SparseCore 0:
  38.7 7.2 reduce-scatter.6
  49.6 56.7 reduce-scatter.8
